TPU v7x, 256 devices: a whole 4x4x8 slice. The times are simulated.
256 devices in a mesh: row: 64 (over x, z, core), rep: 4 (over y).
Axes of the slice: x: 4, y: 4, z: 8, core: 2. Of those that a mesh axis runs over, the one named last changes fastest.
Arguments:
- features: bfloat16 [32768, 128], P(('row', 'rep')), may hold values from -6 to 6
- weight: bfloat16 [128, 256], replicated, may hold values from -0.5 to 0.5
- bias_vector: float32 [256], replicated, may hold values from -3 to 3
- cotangent: bfloat16 [32768, 256], P(('row', 'rep')), may hold values from -6 to 6
- block_tiles: bfloat16 [64, 4, 96, 1, 128, 128], P('row', 'rep'), as said below
- tile_rows: int32 [64, 4, 96, 1], P('row', 'rep'), may hold values from 0 to 3
- tile_columns: int32 [64, 4, 96, 1], P('row', 'rep'), may hold values from 0 to 63
- tile_live: int32 [64, 4, 96, 1], P('row', 'rep'), may hold values from 0 to 1, as said below
Outputs:
- activated: bfloat16 [32768, 256], P(('row', 'rep'))
- grad_features: bfloat16 [32768, 128], P(('row', 'rep'))
- grad_weight: float32 [128, 256], replicated
- grad_bias: float32 [256], replicated
Inputs may be any that keep to these rules, and one draw needn't show every extreme that they name: `block_tiles`: A is symmetric: the tile that a live slot puts at block (i, j) is the transpose of the tile that a live slot puts at block (j, i); every block row has a live diagonal tile. `tile_live`: the number of live slots differs from device to device.
All inputs are finite; a program needn't handle non-finite values.
Results may differ from a plain program's by a relative error of at most 0.0095.
Values may be sent and summed in bfloat16 or wider, within the bound.
No kernel may reach another device: no remote copies, remote signals or barrier semaphores. Data moves between devices by JAX's collectives and lax.ppermute only.
A program may use at most 64 MiB of HBM per device.

v0:
```python
import math

import jax
import jax.numpy as jnp
from jax import lax
from jax.experimental import pallas as pl
from jax.experimental.pallas import tpu as pltpu
from jax.sharding import Mesh, PartitionSpec as P

SLOT_CHUNK = 16


def _agg_kernel(cols_ref, rows_ref, live_ref, tiles_ref, *rest):
    *panel_refs, out_ref = rest
    step = pl.program_id(0)
    chunk = tiles_ref.shape[0]

    @pl.when(step == 0)
    def _():
        out_ref[...] = jnp.zeros_like(out_ref)

    for k in range(chunk):
        slot = step * chunk + k
        column = cols_ref[slot]
        row = rows_ref[slot]
        tile = tiles_ref[k]
        acc = jnp.dot(tile, panel_refs[0][column], preferred_element_type=jnp.float32)
        for panel_ref in panel_refs[1:]:
            acc = acc + jnp.dot(tile, panel_ref[column], preferred_element_type=jnp.float32)
        out_ref[row] += jnp.where(live_ref[slot] != 0, acc, 0.0)


def aggregate(tiles, cols, rows, live, panels, group_rows):
    slot_count, tile_size, _ = tiles.shape
    n_blocks, _, width = panels[0].shape
    chunk = math.gcd(slot_count, SLOT_CHUNK)
    grid_spec = pltpu.PrefetchScalarGridSpec(
        num_scalar_prefetch=3,
        grid=(slot_count // chunk,),
        in_specs=[pl.BlockSpec((chunk, tile_size, tile_size), lambda i, *_: (i, 0, 0))]
        + [pl.BlockSpec((n_blocks, tile_size, width), lambda i, *_: (0, 0, 0)) for _ in panels],
        out_specs=pl.BlockSpec((group_rows, tile_size, width), lambda i, *_: (0, 0, 0)),
    )
    return pl.pallas_call(
        _agg_kernel,
        grid_spec=grid_spec,
        out_shape=jax.ShapeDtypeStruct((group_rows, tile_size, width), jnp.float32),
        compiler_params=pltpu.CompilerParams(dimension_semantics=("arbitrary",)),
    )(cols, rows, live, tiles, *panels)


def gather_a2a(block, axis):
    n = lax.axis_size(axis)
    spread = jnp.broadcast_to(block[None], (n,) + block.shape)
    return lax.all_to_all(spread, axis, 0, 0, tiled=False)


def gather_rows(block):
    return gather_a2a(gather_a2a(gather_a2a(block, "z"), "x"), "core")


def panel_index(cols):
    n_z = lax.axis_size("z")
    n_core = lax.axis_size("core")
    n_x = lax.axis_size("x")
    core = cols % n_core
    z = (cols // n_core) % n_z
    x = cols // (n_core * n_z)
    return (core * n_x + x) * n_z + z


def reduce_rep_a2a(parts):
    received = lax.all_to_all(parts, "rep", 0, 0, tiled=False)
    total = received[0]
    for j in range(1, received.shape[0]):
        total = total + received[j]
    return total


def activate(values):
    return jax.nn.gelu(values, approximate=True)


def split_bf16(values):
    high = values.astype(jnp.bfloat16)
    low = (values - high.astype(jnp.float32)).astype(jnp.bfloat16)
    return high, low


def shards(
    features, weight, bias_vector, cotangent, block_tiles, tile_rows, tile_columns, tile_live
):
    tile_size = block_tiles.shape[-1]
    n_rep = lax.axis_size("rep")
    n_row = lax.axis_size("x") * lax.axis_size("z") * lax.axis_size("core")
    fin = features.shape[1]
    fout = weight.shape[1]
    node_total = features.shape[0] * n_row * n_rep
    group_rows = n_rep * (features.shape[0] // tile_size)
    slot_count = block_tiles.shape[2] * block_tiles.shape[3]
    tiles = block_tiles.reshape(slot_count, tile_size, tile_size)
    rows = tile_rows.reshape(slot_count)
    cols = tile_columns.reshape(slot_count)
    live = tile_live.reshape(slot_count)
    weight_wide = weight.astype(jnp.float32)

    x_panel = gather_rows(features.reshape(-1, tile_size, fin))
    x_panel = x_panel.reshape(n_row, tile_size, fin)
    z_parts = aggregate(tiles, panel_index(cols), rows, live, [x_panel], group_rows)
    z_own = reduce_rep_a2a(z_parts.reshape(n_rep, -1, fin)).reshape(-1, fin)
    hidden = (
        jnp.dot(z_own, weight_wide, precision=lax.Precision.HIGHEST, preferred_element_type=jnp.float32)
        + bias_vector
    )
    activated, pullback = jax.vjp(activate, hidden)
    grad_hidden = pullback(cotangent.astype(jnp.float32))[0]

    joined = jnp.concatenate([z_own, grad_hidden], axis=1)
    joined_all = lax.all_gather(joined, ("x", "z", "core"), axis=0, tiled=True)
    z_quarter = joined_all[:, :fin]
    dh_quarter = joined_all[:, fin:]
    z_high, z_low = split_bf16(z_quarter)
    dh_high, dh_low = split_bf16(dh_quarter)

    def z_t_dot(a, b):
        return lax.dot_general(a, b, (((0,), (0,)), ((), ())), preferred_element_type=jnp.float32)

    weight_term = z_t_dot(z_high, dh_high) + (z_t_dot(z_high, dh_low) + z_t_dot(z_low, dh_high))
    bias_term = jnp.sum(dh_quarter, axis=0)
    pad = (-(fin + 1)) % 8
    terms = jnp.concatenate(
        [weight_term, bias_term[None], jnp.zeros((pad, fout), jnp.float32)], axis=0
    )
    spread = jnp.broadcast_to(terms[None], (n_rep,) + terms.shape)
    totals = reduce_rep_a2a(spread)

    weight_t = weight.T
    p_quarter = jnp.dot(dh_high, weight_t, preferred_element_type=jnp.float32) + jnp.dot(
        dh_low, weight_t, preferred_element_type=jnp.float32
    )
    p_high, p_low = split_bf16(p_quarter.reshape(n_row, tile_size, fin))
    g_parts = aggregate(tiles, cols, rows, live, [p_high, p_low], group_rows)
    grad_features = reduce_rep_a2a(g_parts.reshape(n_rep, -1, fin)).reshape(-1, fin)

    factor = 1.0 / math.sqrt(node_total)
    grad_weight = totals[:fin] * factor
    grad_bias = totals[fin] * factor
    return (activated.astype(jnp.bfloat16), grad_features.astype(jnp.bfloat16), grad_weight, grad_bias)


def solution(mesh):
    n_row = mesh.shape["row"]
    n_core = 2
    n_z = 8 if n_row % (8 * n_core) == 0 else 1
    fine = Mesh(
        mesh.devices.reshape(n_row // (n_z * n_core), n_z, n_core, mesh.shape["rep"]),
        ("x", "z", "core", "rep"),
    )
    row = ("x", "z", "core")
    in_specs = (
        P((*row, "rep"), None),
        P(),
        P(),
        P((*row, "rep"), None),
        P(row, "rep", None, None, None, None),
        P(row, "rep", None, None),
        P(row, "rep", None, None),
        P(row, "rep", None, None),
    )
    out_specs = (P((*row, "rep"), None), P((*row, "rep"), None), P(), P())
    return jax.shard_map(shards, mesh=fine, in_specs=in_specs, out_specs=out_specs, check_vma=False)
```

profile of v0, /device:TPU:1, one launch (start us, length us, event | category | flops | bytes accessed | tf_op | source)
XLA Modules:
  0.0 221.0 jit_solution(3880456111793477392)
XLA Ops:
  7.2 0.0 copy-start
  7.2 0.0 copy-start.2
  7.2 0.8 broadcast_in_dim.16
  8.0 19.3 %all_to_all.30 = bf16[8,1,128,128]{3,2,1,0:T(8,128)(2,1)S(1)} all-to-all(bf16[8,1,128,128]{3,2,1,0:T(8,128)(2,1)S(1)} %broadcast_in_dim.16), channel_id=1, replica_groups=mesh['x'=4,'z'=8,'core'=2,'rep'=4] {'z'}, dimensions={0} | all-to-all | bytes 524288 | tf_op jit(solution)/shard_map/all_to_all | solution.py:55
  27.3 1.2 broadcast_in_dim.36
  28.5 4.0 %all-to-all-start.1 = ((bf16[4,8,1,128,128]{4,3,1,2,0:T(8,128)(2,1)}), bf16[4,8,1,128,128]{4,3,1,2,0:T(8,128)(2,1)S(1)}, u32[]{:S(2)}, u32[]{:S(2)}) async-start(bf16[4,8,1,128,128]{4,3,1,2,0:T(8,128)(2,1)} %broadcast_in_dim.36), calls=%async_computation.1 | async-start | bytes 2097152 | tf_op jit(solution)/shard_map/all_to_all | solution.py:55
  32.6 0.0 all-gather.2.cloned.1.call-start
  32.6 0.0 copy-done.2
  32.6 0.5 fusion.15.cols_ref
  33.1 11.8 %all-to-all-done.1 = bf16[4,8,1,128,128]{4,3,1,2,0:T(8,128)(2,1)S(1)} async-done(((bf16[4,8,1,128,128]{4,3,1,2,0:T(8,128)(2,1)}), bf16[4,8,1,128,128]{4,3,1,2,0:T(8,128)(2,1)S(1)}, u32[]{:S(2)}, u32[]{:S(2)}) %all-to-all-start.1) | async-done | bytes 1048608 | tf_op jit(solution)/shard_map/all_to_all | solution.py:55
  44.8 0.5 broadcast_in_dim.38
  45.3 9.7 %all_to_all.31 = bf16[2,4,8,1,128,128]{5,4,2,1,3,0:T(8,128)(2,1)} all-to-all(bf16[2,4,8,1,128,128]{5,4,2,1,3,0:T(8,128)(2,1)S(1)} %broadcast_in_dim.38), channel_id=1, replica_groups=mesh['x'=4,'z'=8,'core'=2,'rep'=4] {'core'}, dimensions={0} | all-to-all | bytes 4194304 | tf_op jit(solution)/shard_map/all_to_all | solution.py:55
  55.0 0.0 copy-start.3
  55.0 0.0 copy-start.4
  55.0 6.7 %shard_map.111 = f32[4,128,128]{2,1,0:T(8,128)} custom-call(s32[96]{0:T(128)} %fusion.15.cols_ref, s32[96]{0:T(128)} %bitcast.30, s32[96]{0:T(128)} %bitcast.32, bf16[96,128,128]{2,1,0:T(8,128)(2,1)} %bitcast.24, bf16[64,128,128]{2,1,0:T(8,128)(2,1)} %bitcast.26), custom_call_target="tpu_custom_call" | custom-call | tf_op jit(solution)/shard_map/pallas_call | solution.py:44
  61.8 10.0 %all_to_all.32 = f32[4,128,128]{2,1,0:T(8,128)S(1)} all-to-all(f32[4,128,128]{2,1,0:T(8,128)} %shard_map.111), channel_id=1, replica_groups=mesh['x'=4,'z'=8,'core'=2,'rep'=4] {'rep'}, dimensions={0} | all-to-all | bytes 524288 | tf_op jit(solution)/shard_map/all_to_all | solution.py:73
  71.8 0.0 copy-done
  71.8 0.0 copy-done.3
  71.8 0.0 copy-done.4
  71.8 0.9 fusion.3
  72.8 0.7 pad_maximum_fusion
  73.5 0.0 all-gather.2.cloned.1.call-update
  73.5 0.1 pad.2.clone
  73.6 84.7 %all-gather.2.cloned.1.call-done = f32[8192,384]{1,0:T(8,128)} async-done(((f32[128,384]{1,0:T(8,128)}), f32[8192,384]{1,0:T(8,128)}) %all-gather.2.cloned.1.call-update) | async-done | bytes 12582928 | tf_op jit(solution)/shard_map/all_gather | solution.py:119
  158.3 0.0 copy-start.1
  158.3 4.8 %fusion.24 = f32[8192,128]{1,0:T(8,128)S(1)} fusion(bf16[128,256]{1,0:T(8,128)(2,1)S(1)} %copy-done, f32[8192,384]{1,0:T(8,128)} %all-gather.2.cloned.1.call-done), kind=kOutput, calls=%fused_computation.62 | convolution fusion | flops 536870912 | bytes 8454144 | tf_op jit(solution)/shard_map/dot_general | solution.py:138
  163.1 2.2 copy-done.1
  165.3 1.4 convolution_add_fusion
  166.7 3.2 %subtract_convert_fusion.2 = (bf16[64,128,128]{2,1,0:T(8,128)(2,1)}, bf16[64,128,128]{2,1,0:T(8,128)(2,1)}) fusion(f32[64,128,128]{2,1,0:T(8,128)S(1)} %bitcast.23), kind=kLoop, calls=%fused_computation.5 | loop fusion | flops 4194304 | bytes 8388608 | tf_op jit(solution)/shard_map/convert_element_type | solution.py:86
  169.9 7.8 %shard_map.112 = f32[4,128,128]{2,1,0:T(8,128)} custom-call(s32[96]{0:T(128)} %bitcast.35, s32[96]{0:T(128)} %bitcast.31, s32[96]{0:T(128)} %bitcast.33, bf16[96,128,128]{2,1,0:T(8,128)(2,1)} %bitcast.25, bf16[64,128,128]{2,1,0:T(8,128)(2,1)} %get-tuple-element.5.rest_0_, bf16[64,128,128]{2,1,0:T(8,128)(2,1)} %get-tuple-element.4.rest_1_), custom_call_target="tpu_custom_call" | custom-call | tf_op jit(solution)/shard_map/pallas_call | solution.py:44
  177.6 4.0 %all-to-all-start.4 = ((f32[4,128,128]{2,1,0:T(8,128)}), f32[4,128,128]{2,1,0:T(8,128)S(1)}, u32[]{:S(2)}, u32[]{:S(2)}) async-start(f32[4,128,128]{2,1,0:T(8,128)} %shard_map.112), calls=%async_computation.4 | async-start | bytes 524288 | tf_op jit(solution)/shard_map/all_to_all | solution.py:73
  181.6 4.5 %slice_reduce_fusion = f32[256]{0:T(256)S(1)} fusion(f32[8192,384]{1,0:T(8,128)} %all-gather.2.cloned.1.call-done), kind=kLoop, calls=%fused_computation.2 | loop fusion | flops 2096896 | bytes 8389632 | tf_op jit(solution)/shard_map/reduce_sum | solution.py:129
  186.1 0.0 slice-start
  186.1 0.0 slice-start.1
  186.1 5.6 %fusion = f32[128,256]{1,0:T(8,128)S(1)} fusion(f32[8192,384]{1,0:T(8,128)} %all-gather.2.cloned.1.call-done), kind=kOutput, calls=%fused_computation.7 | convolution fusion | flops 541065216 | bytes 8519680 | tf_op jit(solution)/shard_map/dot_general | solution.py:126
  191.7 0.0 slice-start.2
  191.7 5.9 %fusion.19 = f32[128,256]{1,0:T(8,128)S(1)} fusion(f32[8192,384]{1,0:T(8,128)} %all-gather.2.cloned.1.call-done), kind=kOutput, calls=%fused_computation.57 | convolution fusion | flops 536870912 | bytes 6422528 | tf_op jit(solution)/shard_map/dot_general | solution.py:126
  197.7 0.0 slice-done
  197.7 0.0 slice-done.1
  197.7 0.6 slice-done.2
  198.3 0.8 fusion.1
  199.1 0.1 maximum_maximum_fusion
  199.2 0.0 all-to-all-done.4
  199.2 0.9 broadcast_in_dim.41
  200.1 4.2 %all-to-all-start.5 = ((f32[4,136,256]{2,1,0:T(8,128)}), f32[4,136,256]{2,1,0:T(8,128)S(1)}, u32[]{:S(2)}, u32[]{:S(2)}) async-start(f32[4,136,256]{2,1,0:T(8,128)} %broadcast_in_dim.41), calls=%async_computation.5 | async-start | bytes 1114112 | tf_op jit(solution)/shard_map/all_to_all | solution.py:73
  204.3 0.6 fusion.14
  204.9 7.9 %all-to-all-done.5 = f32[4,136,256]{2,1,0:T(8,128)S(1)} async-done(((f32[4,136,256]{2,1,0:T(8,128)}), f32[4,136,256]{2,1,0:T(8,128)S(1)}, u32[]{:S(2)}, u32[]{:S(2)}) %all-to-all-start.5) | async-done | bytes 557088 | tf_op jit(solution)/shard_map/all_to_all | solution.py:73
  212.9 0.6 slice_multiply_fusion.1
  213.5 0.7 fusion.11
  (4 shorter events, 0.1 us)
Async XLA Ops:
  7.2 64.6 %copy-start = (bf16[128,256]{1,0:T(8,128)(2,1)S(1)}, bf16[128,256]{1,0:T(8,128)(2,1)}, u32[]{:S(2)}) copy-start(bf16[128,256]{1,0:T(8,128)(2,1)} %param.9) | copy-start | bytes 196612
  7.2 25.4 %copy-start.2 = (s32[1,1,96,1]{2,3,1,0:T(1,128)S(1)}, s32[1,1,96,1]{2,3,1,0:T(1,128)}, u32[]{:S(2)}) copy-start(s32[1,1,96,1]{2,3,1,0:T(1,128)} %param.14) | copy-start | bytes 1156
  28.5 16.3 %all-to-all-start.1 = ((bf16[4,8,1,128,128]{4,3,1,2,0:T(8,128)(2,1)}), bf16[4,8,1,128,128]{4,3,1,2,0:T(8,128)(2,1)S(1)}, u32[]{:S(2)}, u32[]{:S(2)}) async-start(bf16[4,8,1,128,128]{4,3,1,2,0:T(8,128)(2,1)} %broadcast_in_dim.36), calls=%async_computation.1 | async-start | bytes 2097152 | tf_op jit(solution)/shard_map/all_to_all | solution.py:55
  32.6 125.7 %all-gather.2.cloned.1.call-start = ((), (), s32[]{:S(2)}) async-start(), calls=%async_computation.6 | async-start | bytes 12779520 | tf_op jit(solution)/shard_map/all_gather | solution.py:119
  55.0 16.8 %copy-start.3 = (bf16[128,256]{1,0:T(8,128)(2,1)S(1)}, bf16[128,256]{1,0:T(8,128)(2,1)}, u32[]{:S(2)}) copy-start(bf16[128,256]{1,0:T(8,128)(2,1)} %param.11) | copy-start | bytes 196612
  55.0 16.8 %copy-start.4 = (f32[256]{0:T(256)S(1)}, f32[256]{0:T(256)}, u32[]{:S(2)}) copy-start(f32[256]{0:T(256)} %param.10) | copy-start | bytes 3076
  158.3 7.0 %copy-start.1 = (f32[8192,384]{1,0:T(8,128)S(1)}, f32[8192,384]{1,0:T(8,128)}, u32[]{:S(2)}) copy-start(f32[8192,384]{1,0:T(8,128)} %all-gather.2.cloned.1.call-done) | copy-start | bytes 37748740
  177.6 21.6 %all-to-all-start.4 = ((f32[4,128,128]{2,1,0:T(8,128)}), f32[4,128,128]{2,1,0:T(8,128)S(1)}, u32[]{:S(2)}, u32[]{:S(2)}) async-start(f32[4,128,128]{2,1,0:T(8,128)} %shard_map.112), calls=%async_computation.4 | async-start | bytes 524288 | tf_op jit(solution)/shard_map/all_to_all | solution.py:73
  186.1 11.6 %slice-start = ((s8[12582912]{0:T(1024)(128)(4,1)}), s8[4194304]{0:T(1024)(128)(4,1)S(1)}, s32[]{:S(2)}) async-start(s8[12582912]{0:T(1024)(128)(4,1)} %bitcast.21), calls=%async_computation.7 | async-start | bytes 8388608
  186.1 11.6 %slice-start.1 = ((s8[12582912]{0:T(1024)(128)(4,1)}), s8[4194304]{0:T(1024)(128)(4,1)S(1)}, s32[]{:S(2)}) async-start(s8[12582912]{0:T(1024)(128)(4,1)} %bitcast.21), calls=%async_computation.8 | async-start | bytes 8388608
  191.7 6.6 %slice-start.2 = ((s8[12582912]{0:T(1024)(128)(4,1)}), s8[4194304]{0:T(1024)(128)(4,1)S(1)}, s32[]{:S(2)}) async-start(s8[12582912]{0:T(1024)(128)(4,1)} %bitcast.21), calls=%async_computation.9 | async-start | bytes 8388608
  200.1 12.8 %all-to-all-start.5 = ((f32[4,136,256]{2,1,0:T(8,128)}), f32[4,136,256]{2,1,0:T(8,128)S(1)}, u32[]{:S(2)}, u32[]{:S(2)}) async-start(f32[4,136,256]{2,1,0:T(8,128)} %broadcast_in_dim.41), calls=%async_computation.5 | async-start | bytes 1114112 | tf_op jit(solution)/shard_map/all_to_all | solution.py:73
Sparse Core Ops, SparseCore 0:
  73.6 84.6 all-gather.1
where the time goes:
time: 222 us; the launch traced here: 221 us
  waiting for transfers between devices  104 us (47%)
  blocking collectives  39 us (18%)
  matrix products  19.5 us (9%)
  Pallas kernels  14.5 us (7%)
  between operations  14.2 us (6%)
  starting transfers between devices  12.3 us (6%)
  other arithmetic  10.9 us (5%)
  local copies, waits for them, and re-layouts  6.31 us (3%)
    all_gather x1, waiting for transfers between devices, shards(): joined_all = lax.all_gather(joined, ('x', 'z', 'core'), axis=0, tiled=True)  84.7 us
    all_to_all x2, blocking collectives, gather_a2a(): return lax.all_to_all(spread, axis, 0, 0, tiled=False)  29 us
    pallas_call x2, Pallas kernels, aggregate(): pl.pallas_call(_agg_kernel, grid_spec=grid_spec, out_shape=jax.ShapeDtype...  14.5 us
    dot_general x3, matrix products, z_t_dot(): lax.dot_general(a, b, (((0,), (0,)), ((), ())), preferred_element_type=jn...  12.3 us
    all_to_all x1, waiting for transfers between devices, gather_a2a(): return lax.all_to_all(spread, axis, 0, 0, tiled=False)  11.8 us
    all_to_all x1, blocking collectives, reduce_rep_a2a(): received = lax.all_to_all(parts, 'rep', 0, 0, tiled=False)  9.99 us
    all_to_all x2, starting transfers between devices, reduce_rep_a2a(): received = lax.all_to_all(parts, 'rep', 0, 0, tiled=False)  8.24 us
    all_to_all x2, waiting for transfers between devices, reduce_rep_a2a(): received = lax.all_to_all(parts, 'rep', 0, 0, tiled=False)  7.9 us
  transfers between devices with their start and end apart: 4, of which 3 were waited for; matrix products, arithmetic and copies ran while one was open for 8% of the time, Pallas kernels for 0%

commit v1 on v0

--- a/solution.py
+++ b/solution.py
@@ -104,6 +104,8 @@
     live = tile_live.reshape(slot_count)
     weight_wide = weight.astype(jnp.float32)
 
+    cot_quarter = lax.all_gather(cotangent, ("x", "z", "core"), axis=0, tiled=True)
+
     x_panel = gather_rows(features.reshape(-1, tile_size, fin))
     x_panel = x_panel.reshape(n_row, tile_size, fin)
     z_parts = aggregate(tiles, panel_index(cols), rows, live, [x_panel], group_rows)
@@ -112,13 +114,21 @@
         jnp.dot(z_own, weight_wide, precision=lax.Precision.HIGHEST, preferred_element_type=jnp.float32)
         + bias_vector
     )
-    activated, pullback = jax.vjp(activate, hidden)
-    grad_hidden = pullback(cotangent.astype(jnp.float32))[0]
+    activated = activate(hidden)
 
-    joined = jnp.concatenate([z_own, grad_hidden], axis=1)
-    joined_all = lax.all_gather(joined, ("x", "z", "core"), axis=0, tiled=True)
-    z_quarter = joined_all[:, :fin]
-    dh_quarter = joined_all[:, fin:]
+    z_quarter = gather_rows(z_own).reshape(-1, fin)
+    n_x, n_z, n_core = (lax.axis_size(a) for a in ("x", "z", "core"))
+    cot_quarter = cot_quarter.reshape(n_x, n_z, n_core, -1, fout).transpose(2, 0, 1, 3, 4)
+    cot_quarter = cot_quarter.reshape(-1, fout)
+    zq_high, zq_low = split_bf16(z_quarter)
+    hidden_quarter = (
+        jnp.dot(zq_high, weight, preferred_element_type=jnp.float32)
+        + jnp.dot(zq_low, weight, preferred_element_type=jnp.float32)
+        + bias_vector
+    )
+    _, pullback = jax.vjp(activate, hidden_quarter)
+    dh_quarter = pullback(cot_quarter.astype(jnp.float32))[0]
+    cols = panel_index(cols)
     z_high, z_low = split_bf16(z_quarter)
     dh_high, dh_low = split_bf16(dh_quarter)
 

time: 222 us -> 202 us (0.910)
  waiting for transfers between devices: 104 us -> 45.5 us
  blocking collectives: 39 us -> 71.6 us
  local copies, waits for them, and re-layouts: 6.31 us -> 10.4 us
  other arithmetic: 10.9 us -> 7.52 us
  matrix products: 19.5 us -> 22.2 us
    all_gather x1, waiting for transfers between devices: 84.7 us -> 0.01 us  [shards(): lax.all_gather(cotangent, ('x', 'z', 'core'), axis=0, tiled=True)]
    all_to_all x2 -> x4, blocking collectives: 29 us -> 61.7 us  [gather_a2a(): return lax.all_to_all(spread, axis, 0, 0, tiled=False)]
    all_to_all x1 -> x2, waiting for transfers between devices: 11.8 us -> 36.5 us  [gather_a2a(): return lax.all_to_all(spread, axis, 0, 0, tiled=False)]
    dot_general x0 -> x2, matrix products: none -> 12.9 us  [the longest x1 8.44 us: shards(): jnp.dot(zq_low, weight, preferred_element_type=jnp.float32)]
    dot_general x3, matrix products: 12.3 us -> 5.9 us  [z_t_dot(): lax.dot_general(a, b, (((0,), (0,)), ((), ())), preferred_element_type=jn...]
    reduce_sum x1 -> x0, other arithmetic: 4.47 us -> none  [shards(): bias_term = jnp.sum(dh_quarter, axis=0)]
    all_to_all x1 -> x2, starting transfers between devices: 4.01 us -> 7.62 us  [gather_a2a(): return lax.all_to_all(spread, axis, 0, 0, tiled=False)]
    dot_general x1, matrix products: 4.78 us -> 1.26 us  [shards(): jnp.dot(dh_high, weight_t, preferred_element_type=jnp.float32)]
  transfers between devices with their start and end apart: 4 -> 5, of which waited for: 3 -> 4; matrix products, arithmetic and copies ran while one was open for 8% -> 9% of each run, Pallas kernels for 0% -> 3%
where the time goes in v1:
time: 202 us; the launch traced here: 201 us
  blocking collectives  71.6 us (35%)
  waiting for transfers between devices  45.5 us (23%)
  matrix products  22.2 us (11%)
  Pallas kernels  14.6 us (7%)
  starting transfers between devices  14.5 us (7%)
  between operations  14.2 us (7%)
  local copies, waits for them, and re-layouts  10.4 us (5%)
  other arithmetic  7.52 us (4%)
    all_to_all x4, blocking collectives, gather_a2a(): return lax.all_to_all(spread, axis, 0, 0, tiled=False)  61.7 us
    all_to_all x2, waiting for transfers between devices, gather_a2a(): return lax.all_to_all(spread, axis, 0, 0, tiled=False)  36.5 us
    pallas_call x2, Pallas kernels, aggregate(): pl.pallas_call(_agg_kernel, grid_spec=grid_spec, out_shape=jax.ShapeDtype...  14.6 us
    all_to_all x1, blocking collectives, reduce_rep_a2a(): received = lax.all_to_all(parts, 'rep', 0, 0, tiled=False)  9.98 us
    dot_general x1, matrix products, shards(): jnp.dot(zq_low, weight, preferred_element_type=jnp.float32)  8.44 us
    all_to_all x2, waiting for transfers between devices, reduce_rep_a2a(): received = lax.all_to_all(parts, 'rep', 0, 0, tiled=False)  8.31 us
    all_to_all x2, starting transfers between devices, gather_a2a(): return lax.all_to_all(spread, axis, 0, 0, tiled=False)  7.62 us
    all_to_all x2, starting transfers between devices, reduce_rep_a2a(): received = lax.all_to_all(parts, 'rep', 0, 0, tiled=False)  6.88 us
  transfers between devices with their start and end apart: 5, of which 4 were waited for; matrix products, arithmetic and copies ran while one was open for 9% of the time, Pallas kernels for 3%

profile of v1, /device:TPU:1, one launch (start us, length us, event | category | flops | bytes accessed | tf_op | source)
XLA Modules:
  0.0 200.5 jit_solution(16461024702616662548)
XLA Ops:
  7.2 0.0 copy-start
  7.2 0.0 copy-start.5
  7.2 0.0 all-gather.2.cloned.1.call-start
  7.2 0.7 all-gather.2.cloned.1.call-update
  7.9 0.8 broadcast_in_dim.22
  8.7 19.3 %all_to_all.45 = bf16[8,1,128,128]{3,2,1,0:T(8,128)(2,1)S(1)} all-to-all(bf16[8,1,128,128]{3,2,1,0:T(8,128)(2,1)S(1)} %broadcast_in_dim.22), channel_id=1, replica_groups=mesh['x'=4,'z'=8,'core'=2,'rep'=4] {'z'}, dimensions={0} | all-to-all | bytes 524288 | tf_op jit(solution)/shard_map/all_to_all | solution.py:55
  28.0 1.2 broadcast_in_dim.24
  29.2 4.0 %all-to-all-start.1 = ((bf16[4,8,1,128,128]{4,3,1,2,0:T(8,128)(2,1)}), bf16[4,8,1,128,128]{4,3,1,2,0:T(8,128)(2,1)S(1)}, u32[]{:S(2)}, u32[]{:S(2)}) async-start(bf16[4,8,1,128,128]{4,3,1,2,0:T(8,128)(2,1)} %broadcast_in_dim.24), calls=%async_computation.1 | async-start | bytes 2097152 | tf_op jit(solution)/shard_map/all_to_all | solution.py:55
  33.3 0.0 copy-done.5
  33.3 0.5 fusion.24.cols_ref
  33.8 12.2 %all-to-all-done.1 = bf16[4,8,1,128,128]{4,3,1,2,0:T(8,128)(2,1)S(1)} async-done(((bf16[4,8,1,128,128]{4,3,1,2,0:T(8,128)(2,1)}), bf16[4,8,1,128,128]{4,3,1,2,0:T(8,128)(2,1)S(1)}, u32[]{:S(2)}, u32[]{:S(2)}) %all-to-all-start.1) | async-done | bytes 1048608 | tf_op jit(solution)/shard_map/all_to_all | solution.py:55
  46.0 0.5 broadcast_in_dim.26
  46.5 9.6 %all_to_all.46 = bf16[2,4,8,1,128,128]{5,4,2,1,3,0:T(8,128)(2,1)} all-to-all(bf16[2,4,8,1,128,128]{5,4,2,1,3,0:T(8,128)(2,1)S(1)} %broadcast_in_dim.26), channel_id=1, replica_groups=mesh['x'=4,'z'=8,'core'=2,'rep'=4] {'core'}, dimensions={0} | all-to-all | bytes 4194304 | tf_op jit(solution)/shard_map/all_to_all | solution.py:55
  56.1 6.6 %shard_map.111 = f32[4,128,128]{2,1,0:T(8,128)} custom-call(s32[96]{0:T(128)} %fusion.24.cols_ref, s32[96]{0:T(128)} %bitcast.72, s32[96]{0:T(128)} %bitcast.74, bf16[96,128,128]{2,1,0:T(8,128)(2,1)} %bitcast.66, bf16[64,128,128]{2,1,0:T(8,128)(2,1)} %bitcast.68), custom_call_target="tpu_custom_call" | custom-call | tf_op jit(solution)/shard_map/pallas_call | solution.py:44
  62.7 10.0 %all_to_all.47 = f32[4,128,128]{2,1,0:T(8,128)S(1)} all-to-all(f32[4,128,128]{2,1,0:T(8,128)} %shard_map.111), channel_id=1, replica_groups=mesh['x'=4,'z'=8,'core'=2,'rep'=4] {'rep'}, dimensions={0} | all-to-all | bytes 524288 | tf_op jit(solution)/shard_map/all_to_all | solution.py:73
  72.8 23.2 %all_to_all.48 = f32[8,128,128]{2,1,0:T(8,128)S(1)} all-to-all(f32[8,128,128]{2,1,0:T(8,128)S(1)} %broadcast_in_dim.27), channel_id=1, replica_groups=mesh['x'=4,'z'=8,'core'=2,'rep'=4] {'z'}, dimensions={0} | all-to-all | bytes 1048576 | tf_op jit(solution)/shard_map/all_to_all | solution.py:55
  95.9 1.6 broadcast_in_dim.28
  97.5 3.6 %all-to-all-start.5 = ((f32[4,8,128,128]{3,2,1,0:T(8,128)}), f32[4,8,128,128]{3,2,1,0:T(8,128)S(1)}, u32[]{:S(2)}, u32[]{:S(2)}) async-start(f32[4,8,128,128]{3,2,1,0:T(8,128)} %broadcast_in_dim.28), calls=%async_computation.5 | async-start | bytes 4194304 | tf_op jit(solution)/shard_map/all_to_all | solution.py:55
  101.1 0.1 pad.2.clone
  101.2 24.3 %all-to-all-done.5 = f32[4,8,128,128]{3,2,1,0:T(8,128)S(1)} async-done(((f32[4,8,128,128]{3,2,1,0:T(8,128)}), f32[4,8,128,128]{3,2,1,0:T(8,128)S(1)}, u32[]{:S(2)}, u32[]{:S(2)}) %all-to-all-start.5) | async-done | bytes 2097184 | tf_op jit(solution)/shard_map/all_to_all | solution.py:55
  125.5 0.5 broadcast_in_dim.29
  126.0 9.6 %all_to_all.49 = f32[2,4,8,128,128]{4,3,2,1,0:T(8,128)S(1)} all-to-all(f32[2,4,8,128,128]{4,3,2,1,0:T(8,128)S(1)} %broadcast_in_dim.29), channel_id=1, replica_groups=mesh['x'=4,'z'=8,'core'=2,'rep'=4] {'core'}, dimensions={0} | all-to-all | bytes 8388608 | tf_op jit(solution)/shard_map/all_to_all | solution.py:55
  135.6 1.9 fusion.10
  137.5 0.0 copy-done
  137.5 4.5 %fusion.37 = f32[8192,256]{1,0:T(8,128)} fusion(bf16[8192,128]{1,0:T(8,128)(2,1)S(1)} %get-tuple-element.7, bf16[128,256]{1,0:T(8,128)(2,1)S(1)} %copy-done), kind=kOutput, calls=%fused_computation.75 | convolution fusion | flops 536870912 | bytes 10551296 | tf_op jit(solution)/shard_map/dot_general | solution.py:125
  142.0 0.0 all-gather.2.cloned.1.call-done
  142.0 0.0 copy-start.2
  142.0 0.0 copy-start.4
  142.0 3.5 %copy.13 = f32[4,8,2,128,256]{4,3,1,0,2:T(8,128)S(1)} copy(bf16[4,8,2,128,256]{4,3,2,1,0:T(8,128)(2,1)} %bitcast.69) | data formatting | bytes 12582912 | tf_op jit(solution)/shard_map/convert_element_type | solution.py:130
  145.5 1.2 copy-done.2
  146.6 0.0 copy-done.4
  146.6 8.4 %fusion.36 = (f32[256]{0:T(256)S(1)}, f32[8192,256]{1,0:T(8,128)S(1)}) fusion(f32[256]{0:T(256)S(1)} %copy-done.4, f32[8192,256]{1,0:T(8,128)S(1)} %copy-done.2, bf16[8192,128]{1,0:T(8,128)(2,1)} %get-tuple-element.6, bf16[128,256]{1,0:T(8,128)(2,1)S(1)} %copy-done, f32[4,8,2,128,256]{4,3,1,0,2:T(8,128)S(1)} %copy.13), kind=kOutput, calls=%fused_computation.74 | convolution fusion | flops 583008000 | bytes 27330560 | tf_op jit(solution)/shard_map/dot_general | solution.py:126
  155.1 0.0 copy-start.1
  155.1 0.9 fusion.28
  156.0 0.9 fusion.31
  156.8 1.3 fusion.34
  158.1 0.2 copy-done.1
  158.3 1.2 convolution_add_fusion.1
  159.5 3.1 %subtract_convert_fusion.1 = (bf16[64,128,128]{2,1,0:T(8,128)(2,1)}, bf16[64,128,128]{2,1,0:T(8,128)(2,1)}) fusion(f32[64,128,128]{2,1,0:T(8,128)S(1)} %bitcast.65), kind=kLoop, calls=%fused_computation.20 | loop fusion | flops 4194304 | bytes 8388608 | tf_op jit(solution)/shard_map/convert_element_type | solution.py:86
  162.7 0.0 copy-start.3
  162.7 7.9 %shard_map.112 = f32[4,128,128]{2,1,0:T(8,128)} custom-call(s32[96]{0:T(128)} %fusion.24.cols_ref, s32[96]{0:T(128)} %bitcast.73, s32[96]{0:T(128)} %bitcast.75, bf16[96,128,128]{2,1,0:T(8,128)(2,1)} %bitcast.67, bf16[64,128,128]{2,1,0:T(8,128)(2,1)} %get-tuple-element.5.rest_0_, bf16[64,128,128]{2,1,0:T(8,128)(2,1)} %get-tuple-element.4.rest_1_), custom_call_target="tpu_custom_call" | custom-call | tf_op jit(solution)/shard_map/pallas_call | solution.py:44
  170.6 3.4 %all-to-all-start.7 = ((f32[4,128,128]{2,1,0:T(8,128)}), f32[4,128,128]{2,1,0:T(8,128)S(1)}, u32[]{:S(2)}, u32[]{:S(2)}) async-start(f32[4,128,128]{2,1,0:T(8,128)} %shard_map.112), calls=%async_computation.7 | async-start | bytes 524288 | tf_op jit(solution)/shard_map/all_to_all | solution.py:73
  174.0 0.0 copy-done.3
  174.0 4.2 %fusion.11 = f32[128,256]{1,0:T(8,128)S(1)} fusion(f32[128,256]{1,0:T(8,128)S(1)} %fusion.31, f32[128,256]{1,0:T(8,128)S(1)} %fusion.28, bf16[8192,128]{1,0:T(8,128)(2,1)S(1)} %copy-done.3, f32[8192,256]{1,0:T(8,128)} %copy-done.1), kind=kOutput, calls=%fused_computation.22 | convolution fusion | flops 539033600 | bytes 10878976 | tf_op jit(solution)/shard_map/dot_general | solution.py:136
  178.2 0.1 maximum_maximum_fusion
  178.3 1.8 all-to-all-done.7
  180.0 0.8 broadcast_in_dim.63
  180.9 3.5 %all-to-all-start.8 = ((f32[4,136,256]{2,1,0:T(8,128)}), f32[4,136,256]{2,1,0:T(8,128)S(1)}, u32[]{:S(2)}, u32[]{:S(2)}) async-start(f32[4,136,256]{2,1,0:T(8,128)} %broadcast_in_dim.63), calls=%async_computation.8 | async-start | bytes 1114112 | tf_op jit(solution)/shard_map/all_to_all | solution.py:73
  184.4 0.9 fusion.19
  185.2 0.6 fusion.23
  185.9 6.5 %all-to-all-done.8 = f32[4,136,256]{2,1,0:T(8,128)S(1)} async-done(((f32[4,136,256]{2,1,0:T(8,128)}), f32[4,136,256]{2,1,0:T(8,128)S(1)}, u32[]{:S(2)}, u32[]{:S(2)}) %all-to-all-start.8) | async-done | bytes 557088 | tf_op jit(solution)/shard_map/all_to_all | solution.py:73
  192.5 0.6 slice_multiply_fusion.1
  193.0 0.7 fusion.20
  (4 shorter events, 0.1 us)
Async XLA Ops:
  7.2 130.3 %copy-start = (bf16[128,256]{1,0:T(8,128)(2,1)S(1)}, bf16[128,256]{1,0:T(8,128)(2,1)}, u32[]{:S(2)}) copy-start(bf16[128,256]{1,0:T(8,128)(2,1)} %param.9) | copy-start | bytes 196612
  7.2 26.1 %copy-start.5 = (s32[1,1,96,1]{2,3,1,0:T(1,128)S(1)}, s32[1,1,96,1]{2,3,1,0:T(1,128)}, u32[]{:S(2)}) copy-start(s32[1,1,96,1]{2,3,1,0:T(1,128)} %param.14) | copy-start | bytes 1156
  7.2 134.8 %all-gather.2.cloned.1.call-start = ((), (), s32[]{:S(2)}) async-start(), calls=%async_computation.9 | async-start | bytes 4259840 | tf_op jit(solution)/shard_map/all_gather | solution.py:107
  29.2 16.8 %all-to-all-start.1 = ((bf16[4,8,1,128,128]{4,3,1,2,0:T(8,128)(2,1)}), bf16[4,8,1,128,128]{4,3,1,2,0:T(8,128)(2,1)S(1)}, u32[]{:S(2)}, u32[]{:S(2)}) async-start(bf16[4,8,1,128,128]{4,3,1,2,0:T(8,128)(2,1)} %broadcast_in_dim.24), calls=%async_computation.1 | async-start | bytes 2097152 | tf_op jit(solution)/shard_map/all_to_all | solution.py:55
  97.5 28.0 %all-to-all-start.5 = ((f32[4,8,128,128]{3,2,1,0:T(8,128)}), f32[4,8,128,128]{3,2,1,0:T(8,128)S(1)}, u32[]{:S(2)}, u32[]{:S(2)}) async-start(f32[4,8,128,128]{3,2,1,0:T(8,128)} %broadcast_in_dim.28), calls=%async_computation.5 | async-start | bytes 4194304 | tf_op jit(solution)/shard_map/all_to_all | solution.py:55
  142.0 4.6 %copy-start.2 = (f32[8192,256]{1,0:T(8,128)S(1)}, f32[8192,256]{1,0:T(8,128)}, u32[]{:S(2)}) copy-start(f32[8192,256]{1,0:T(8,128)} %fusion.37) | copy-start | bytes 25165828
  142.0 4.6 %copy-start.4 = (f32[256]{0:T(256)S(1)}, f32[256]{0:T(256)}, u32[]{:S(2)}) copy-start(f32[256]{0:T(256)} %param.10) | copy-start | bytes 3076
  155.1 3.2 %copy-start.1 = (f32[8192,256]{1,0:T(8,128)}, f32[8192,256]{1,0:T(8,128)S(1)}, u32[]{:S(2)}) copy-start(f32[8192,256]{1,0:T(8,128)S(1)} %get-tuple-element.9) | copy-start | bytes 25165828
  162.7 11.4 %copy-start.3 = (bf16[8192,128]{1,0:T(8,128)(2,1)S(1)}, bf16[8192,128]{1,0:T(8,128)(2,1)}, u32[]{:S(2)}) copy-start(bf16[8192,128]{1,0:T(8,128)(2,1)} %get-tuple-element.6) | copy-start | bytes 6291460
  170.6 9.4 %all-to-all-start.7 = ((f32[4,128,128]{2,1,0:T(8,128)}), f32[4,128,128]{2,1,0:T(8,128)S(1)}, u32[]{:S(2)}, u32[]{:S(2)}) async-start(f32[4,128,128]{2,1,0:T(8,128)} %shard_map.112), calls=%async_computation.7 | async-start | bytes 524288 | tf_op jit(solution)/shard_map/all_to_all | solution.py:73
  180.9 11.5 %all-to-all-start.8 = ((f32[4,136,256]{2,1,0:T(8,128)}), f32[4,136,256]{2,1,0:T(8,128)S(1)}, u32[]{:S(2)}, u32[]{:S(2)}) async-start(f32[4,136,256]{2,1,0:T(8,128)} %broadcast_in_dim.63), calls=%async_computation.8 | async-start | bytes 1114112 | tf_op jit(solution)/shard_map/all_to_all | solution.py:73
Sparse Core Ops, SparseCore 0:
  10.8 86.0 all-gather.1

commit v2 on v1

--- a/solution.py
+++ b/solution.py
@@ -6,6 +6,7 @@
 from jax.experimental import pallas as pl
 from jax.experimental.pallas import tpu as pltpu
 from jax.sharding import Mesh, PartitionSpec as P
+
 
 SLOT_CHUNK = 16
 
@@ -87,7 +88,7 @@
     return high, low
 
 
-def shards(
+def layer(
     features, weight, bias_vector, cotangent, block_tiles, tile_rows, tile_columns, tile_live
 ):
     tile_size = block_tiles.shape[-1]
@@ -104,7 +105,7 @@
     live = tile_live.reshape(slot_count)
     weight_wide = weight.astype(jnp.float32)
 
-    cot_quarter = lax.all_gather(cotangent, ("x", "z", "core"), axis=0, tiled=True)
+    cot_quarter = lax.all_gather(cotangent, ("core", "x", "z"), axis=0, tiled=True)
 
     x_panel = gather_rows(features.reshape(-1, tile_size, fin))
     x_panel = x_panel.reshape(n_row, tile_size, fin)
@@ -117,9 +118,6 @@
     activated = activate(hidden)
 
     z_quarter = gather_rows(z_own).reshape(-1, fin)
-    n_x, n_z, n_core = (lax.axis_size(a) for a in ("x", "z", "core"))
-    cot_quarter = cot_quarter.reshape(n_x, n_z, n_core, -1, fout).transpose(2, 0, 1, 3, 4)
-    cot_quarter = cot_quarter.reshape(-1, fout)
     zq_high, zq_low = split_bf16(z_quarter)
     hidden_quarter = (
         jnp.dot(zq_high, weight, preferred_element_type=jnp.float32)
@@ -141,6 +139,7 @@
     terms = jnp.concatenate(
         [weight_term, bias_term[None], jnp.zeros((pad, fout), jnp.float32)], axis=0
     )
+
     spread = jnp.broadcast_to(terms[None], (n_rep,) + terms.shape)
     totals = reduce_rep_a2a(spread)
 
@@ -178,4 +177,4 @@
         P(row, "rep", None, None),
     )
     out_specs = (P((*row, "rep"), None), P((*row, "rep"), None), P(), P())
-    return jax.shard_map(shards, mesh=fine, in_specs=in_specs, out_specs=out_specs, check_vma=False)
+    return jax.shard_map(layer, mesh=fine, in_specs=in_specs, out_specs=out_specs, check_vma=False)

time: 202 us -> 199 us (0.985)
  local copies, waits for them, and re-layouts: 10.4 us -> 5.77 us
    convert_element_type x1 -> x0, local copies, waits for them, and re-layouts: 3.47 us -> none  [shards(): dh_quarter = pullback(cot_quarter.astype(jnp.float32))[0]]
where the time goes in v2:
time: 199 us; the launch traced here: 198 us
  blocking collectives  71.7 us (36%)
  waiting for transfers between devices  45.8 us (23%)
  matrix products  24 us (12%)
  Pallas kernels  14.6 us (7%)
  starting transfers between devices  14.5 us (7%)
  between operations  14.2 us (7%)
  other arithmetic  7.53 us (4%)
  local copies, waits for them, and re-layouts  5.77 us (3%)
    all_to_all x4, blocking collectives, gather_a2a(): return lax.all_to_all(spread, axis, 0, 0, tiled=False)  61.7 us
    all_to_all x2, waiting for transfers between devices, gather_a2a(): return lax.all_to_all(spread, axis, 0, 0, tiled=False)  36.6 us
    pallas_call x2, Pallas kernels, aggregate(): pl.pallas_call(_agg_kernel, grid_spec=grid_spec, out_shape=jax.ShapeDtype...  14.6 us
    dot_general x1, matrix products, layer(): jnp.dot(zq_low, weight, preferred_element_type=jnp.float32)  10.3 us
    all_to_all x1, blocking collectives, reduce_rep_a2a(): received = lax.all_to_all(parts, 'rep', 0, 0, tiled=False)  10 us
    all_to_all x2, waiting for transfers between devices, reduce_rep_a2a(): received = lax.all_to_all(parts, 'rep', 0, 0, tiled=False)  8.46 us
    all_to_all x2, starting transfers between devices, gather_a2a(): return lax.all_to_all(spread, axis, 0, 0, tiled=False)  7.62 us
    all_to_all x2, starting transfers between devices, reduce_rep_a2a(): received = lax.all_to_all(parts, 'rep', 0, 0, tiled=False)  6.88 us
  transfers between devices with their start and end apart: 5, of which 4 were waited for; matrix products, arithmetic and copies ran while one was open for 9% of the time, Pallas kernels for 3%

profile of v2, /device:TPU:1, one launch (start us, length us, event | category | flops | bytes accessed | tf_op | source)
XLA Modules:
  0.0 198.1 jit_solution(35846741861595684)
XLA Ops:
  7.2 0.0 copy-start
  7.2 0.0 copy-start.4
  7.2 0.0 all-gather.2.cloned.1.call-start
  7.2 0.7 all-gather.2.cloned.1.call-update
  7.9 0.8 broadcast_in_dim.22
  8.7 19.3 %all_to_all.45 = bf16[8,1,128,128]{3,2,1,0:T(8,128)(2,1)S(1)} all-to-all(bf16[8,1,128,128]{3,2,1,0:T(8,128)(2,1)S(1)} %broadcast_in_dim.22), channel_id=1, replica_groups=mesh['x'=4,'z'=8,'core'=2,'rep'=4] {'z'}, dimensions={0} | all-to-all | bytes 524288 | tf_op jit(solution)/shard_map/all_to_all | solution.py:56
  28.0 1.2 broadcast_in_dim.24
  29.2 4.0 %all-to-all-start.1 = ((bf16[4,8,1,128,128]{4,3,1,2,0:T(8,128)(2,1)}), bf16[4,8,1,128,128]{4,3,1,2,0:T(8,128)(2,1)S(1)}, u32[]{:S(2)}, u32[]{:S(2)}) async-start(bf16[4,8,1,128,128]{4,3,1,2,0:T(8,128)(2,1)} %broadcast_in_dim.24), calls=%async_computation.1 | async-start | bytes 2097152 | tf_op jit(solution)/shard_map/all_to_all | solution.py:56
  33.2 0.0 copy-done.4
  33.3 0.5 fusion.24.cols_ref
  33.8 12.2 %all-to-all-done.1 = bf16[4,8,1,128,128]{4,3,1,2,0:T(8,128)(2,1)S(1)} async-done(((bf16[4,8,1,128,128]{4,3,1,2,0:T(8,128)(2,1)}), bf16[4,8,1,128,128]{4,3,1,2,0:T(8,128)(2,1)S(1)}, u32[]{:S(2)}, u32[]{:S(2)}) %all-to-all-start.1) | async-done | bytes 1048608 | tf_op jit(solution)/shard_map/all_to_all | solution.py:56
  46.0 0.5 broadcast_in_dim.26
  46.5 9.6 %all_to_all.46 = bf16[2,4,8,1,128,128]{5,4,2,1,3,0:T(8,128)(2,1)} all-to-all(bf16[2,4,8,1,128,128]{5,4,2,1,3,0:T(8,128)(2,1)S(1)} %broadcast_in_dim.26), channel_id=1, replica_groups=mesh['x'=4,'z'=8,'core'=2,'rep'=4] {'core'}, dimensions={0} | all-to-all | bytes 4194304 | tf_op jit(solution)/shard_map/all_to_all | solution.py:56
  56.1 6.6 %shard_map.111 = f32[4,128,128]{2,1,0:T(8,128)} custom-call(s32[96]{0:T(128)} %fusion.24.cols_ref, s32[96]{0:T(128)} %bitcast.54, s32[96]{0:T(128)} %bitcast.56, bf16[96,128,128]{2,1,0:T(8,128)(2,1)} %bitcast.49, bf16[64,128,128]{2,1,0:T(8,128)(2,1)} %bitcast.51), custom_call_target="tpu_custom_call" | custom-call | tf_op jit(solution)/shard_map/pallas_call | solution.py:45
  62.7 10.0 %all_to_all.47 = f32[4,128,128]{2,1,0:T(8,128)S(1)} all-to-all(f32[4,128,128]{2,1,0:T(8,128)} %shard_map.111), channel_id=1, replica_groups=mesh['x'=4,'z'=8,'core'=2,'rep'=4] {'rep'}, dimensions={0} | all-to-all | bytes 524288 | tf_op jit(solution)/shard_map/all_to_all | solution.py:74
  72.8 23.3 %all_to_all.48 = f32[8,128,128]{2,1,0:T(8,128)S(1)} all-to-all(f32[8,128,128]{2,1,0:T(8,128)S(1)} %broadcast_in_dim.27), channel_id=1, replica_groups=mesh['x'=4,'z'=8,'core'=2,'rep'=4] {'z'}, dimensions={0} | all-to-all | bytes 1048576 | tf_op jit(solution)/shard_map/all_to_all | solution.py:56
  96.1 1.6 broadcast_in_dim.28
  97.6 3.6 %all-to-all-start.5 = ((f32[4,8,128,128]{3,2,1,0:T(8,128)}), f32[4,8,128,128]{3,2,1,0:T(8,128)S(1)}, u32[]{:S(2)}, u32[]{:S(2)}) async-start(f32[4,8,128,128]{3,2,1,0:T(8,128)} %broadcast_in_dim.28), calls=%async_computation.5 | async-start | bytes 4194304 | tf_op jit(solution)/shard_map/all_to_all | solution.py:56
  101.3 0.1 pad.2.clone
  101.3 24.4 %all-to-all-done.5 = f32[4,8,128,128]{3,2,1,0:T(8,128)S(1)} async-done(((f32[4,8,128,128]{3,2,1,0:T(8,128)}), f32[4,8,128,128]{3,2,1,0:T(8,128)S(1)}, u32[]{:S(2)}, u32[]{:S(2)}) %all-to-all-start.5) | async-done | bytes 2097184 | tf_op jit(solution)/shard_map/all_to_all | solution.py:56
  125.8 0.5 broadcast_in_dim.29
  126.3 9.5 %all_to_all.49 = f32[2,4,8,128,128]{4,3,2,1,0:T(8,128)S(1)} all-to-all(f32[2,4,8,128,128]{4,3,2,1,0:T(8,128)S(1)} %broadcast_in_dim.29), channel_id=1, replica_groups=mesh['x'=4,'z'=8,'core'=2,'rep'=4] {'core'}, dimensions={0} | all-to-all | bytes 8388608 | tf_op jit(solution)/shard_map/all_to_all | solution.py:56
  135.8 1.9 fusion.10
  137.7 0.0 copy-done
  137.7 0.0 copy-start.3
  137.7 4.5 %fusion.37 = f32[8192,256]{1,0:T(8,128)} fusion(bf16[8192,128]{1,0:T(8,128)(2,1)S(1)} %get-tuple-element.7, bf16[128,256]{1,0:T(8,128)(2,1)S(1)} %copy-done), kind=kOutput, calls=%fused_computation.75 | convolution fusion | flops 536870912 | bytes 10551296 | tf_op jit(solution)/shard_map/dot_general | solution.py:123
  142.1 0.0 all-gather.2.cloned.1.call-done
  142.1 0.0 copy-done.3
  142.2 10.3 %fusion.36 = (f32[256]{0:T(256)S(1)}, f32[8192,256]{1,0:T(8,128)S(1)}) fusion(f32[256]{0:T(256)S(1)} %copy-done.3, f32[8192,256]{1,0:T(8,128)} %fusion.37, bf16[8192,128]{1,0:T(8,128)(2,1)} %get-tuple-element.6, bf16[128,256]{1,0:T(8,128)(2,1)S(1)} %copy-done, bf16[8192,256]{1,0:T(8,128)(2,1)} %all-gather.2.cloned.1.call-done), kind=kOutput, calls=%fused_computation.74 | convolution fusion | flops 585105152 | bytes 23136256 | tf_op jit(solution)/shard_map/dot_general | solution.py:124
  152.5 0.0 copy-start.1
  152.5 0.9 fusion.28
  153.4 0.9 fusion.31
  154.2 1.2 fusion.34
  155.5 0.2 copy-done.1
  155.7 1.2 convolution_add_fusion.1
  157.0 3.1 %subtract_convert_fusion.1 = (bf16[64,128,128]{2,1,0:T(8,128)(2,1)}, bf16[64,128,128]{2,1,0:T(8,128)(2,1)}) fusion(f32[64,128,128]{2,1,0:T(8,128)S(1)} %bitcast.48), kind=kLoop, calls=%fused_computation.20 | loop fusion | flops 4194304 | bytes 8388608 | tf_op jit(solution)/shard_map/convert_element_type | solution.py:87
  160.1 0.0 copy-start.2
  160.1 8.0 %shard_map.112 = f32[4,128,128]{2,1,0:T(8,128)} custom-call(s32[96]{0:T(128)} %fusion.24.cols_ref, s32[96]{0:T(128)} %bitcast.55, s32[96]{0:T(128)} %bitcast.57, bf16[96,128,128]{2,1,0:T(8,128)(2,1)} %bitcast.50, bf16[64,128,128]{2,1,0:T(8,128)(2,1)} %get-tuple-element.5.rest_0_, bf16[64,128,128]{2,1,0:T(8,128)(2,1)} %get-tuple-element.4.rest_1_), custom_call_target="tpu_custom_call" | custom-call | tf_op jit(solution)/shard_map/pallas_call | solution.py:45
  168.0 3.4 %all-to-all-start.7 = ((f32[4,128,128]{2,1,0:T(8,128)}), f32[4,128,128]{2,1,0:T(8,128)S(1)}, u32[]{:S(2)}, u32[]{:S(2)}) async-start(f32[4,128,128]{2,1,0:T(8,128)} %shard_map.112), calls=%async_computation.7 | async-start | bytes 524288 | tf_op jit(solution)/shard_map/all_to_all | solution.py:74
  171.4 0.0 copy-done.2
  171.5 4.2 %fusion.11 = f32[128,256]{1,0:T(8,128)S(1)} fusion(f32[128,256]{1,0:T(8,128)S(1)} %fusion.31, f32[128,256]{1,0:T(8,128)S(1)} %fusion.28, bf16[8192,128]{1,0:T(8,128)(2,1)S(1)} %copy-done.2, f32[8192,256]{1,0:T(8,128)} %copy-done.1), kind=kOutput, calls=%fused_computation.22 | convolution fusion | flops 539033600 | bytes 10878976 | tf_op jit(solution)/shard_map/dot_general | solution.py:134
  175.6 0.1 maximum_maximum_fusion
  175.7 1.8 all-to-all-done.7
  177.6 0.8 broadcast_in_dim.63
  178.4 3.5 %all-to-all-start.8 = ((f32[4,136,256]{2,1,0:T(8,128)}), f32[4,136,256]{2,1,0:T(8,128)S(1)}, u32[]{:S(2)}, u32[]{:S(2)}) async-start(f32[4,136,256]{2,1,0:T(8,128)} %broadcast_in_dim.63), calls=%async_computation.8 | async-start | bytes 1114112 | tf_op jit(solution)/shard_map/all_to_all | solution.py:74
  181.9 0.9 fusion.19
  182.8 0.6 fusion.23
  183.4 6.6 %all-to-all-done.8 = f32[4,136,256]{2,1,0:T(8,128)S(1)} async-done(((f32[4,136,256]{2,1,0:T(8,128)}), f32[4,136,256]{2,1,0:T(8,128)S(1)}, u32[]{:S(2)}, u32[]{:S(2)}) %all-to-all-start.8) | async-done | bytes 557088 | tf_op jit(solution)/shard_map/all_to_all | solution.py:74
  190.0 0.7 fusion.20
  190.7 0.6 slice_multiply_fusion.1
  (4 shorter events, 0.1 us)
Async XLA Ops:
  7.2 130.5 %copy-start = (bf16[128,256]{1,0:T(8,128)(2,1)S(1)}, bf16[128,256]{1,0:T(8,128)(2,1)}, u32[]{:S(2)}) copy-start(bf16[128,256]{1,0:T(8,128)(2,1)} %param.9) | copy-start | bytes 196612
  7.2 26.1 %copy-start.4 = (s32[1,1,96,1]{2,3,1,0:T(1,128)S(1)}, s32[1,1,96,1]{2,3,1,0:T(1,128)}, u32[]{:S(2)}) copy-start(s32[1,1,96,1]{2,3,1,0:T(1,128)} %param.14) | copy-start | bytes 1156
  7.2 135.0 %all-gather.2.cloned.1.call-start = ((), (), s32[]{:S(2)}) async-start(), calls=%async_computation.9 | async-start | bytes 4259840 | tf_op jit(solution)/shard_map/all_gather | solution.py:108
  29.2 16.7 %all-to-all-start.1 = ((bf16[4,8,1,128,128]{4,3,1,2,0:T(8,128)(2,1)}), bf16[4,8,1,128,128]{4,3,1,2,0:T(8,128)(2,1)S(1)}, u32[]{:S(2)}, u32[]{:S(2)}) async-start(bf16[4,8,1,128,128]{4,3,1,2,0:T(8,128)(2,1)} %broadcast_in_dim.24), calls=%async_computation.1 | async-start | bytes 2097152 | tf_op jit(solution)/shard_map/all_to_all | solution.py:56
  97.6 28.1 %all-to-all-start.5 = ((f32[4,8,128,128]{3,2,1,0:T(8,128)}), f32[4,8,128,128]{3,2,1,0:T(8,128)S(1)}, u32[]{:S(2)}, u32[]{:S(2)}) async-start(f32[4,8,128,128]{3,2,1,0:T(8,128)} %broadcast_in_dim.28), calls=%async_computation.5 | async-start | bytes 4194304 | tf_op jit(solution)/shard_map/all_to_all | solution.py:56
  137.7 4.5 %copy-start.3 = (f32[256]{0:T(256)S(1)}, f32[256]{0:T(256)}, u32[]{:S(2)}) copy-start(f32[256]{0:T(256)} %param.10) | copy-start | bytes 3076
  152.5 3.2 %copy-start.1 = (f32[8192,256]{1,0:T(8,128)}, f32[8192,256]{1,0:T(8,128)S(1)}, u32[]{:S(2)}) copy-start(f32[8192,256]{1,0:T(8,128)S(1)} %get-tuple-element.9) | copy-start | bytes 25165828
  160.1 11.4 %copy-start.2 = (bf16[8192,128]{1,0:T(8,128)(2,1)S(1)}, bf16[8192,128]{1,0:T(8,128)(2,1)}, u32[]{:S(2)}) copy-start(bf16[8192,128]{1,0:T(8,128)(2,1)} %get-tuple-element.6) | copy-start | bytes 6291460
  168.0 9.5 %all-to-all-start.7 = ((f32[4,128,128]{2,1,0:T(8,128)}), f32[4,128,128]{2,1,0:T(8,128)S(1)}, u32[]{:S(2)}, u32[]{:S(2)}) async-start(f32[4,128,128]{2,1,0:T(8,128)} %shard_map.112), calls=%async_computation.7 | async-start | bytes 524288 | tf_op jit(solution)/shard_map/all_to_all | solution.py:74
  178.4 11.6 %all-to-all-start.8 = ((f32[4,136,256]{2,1,0:T(8,128)}), f32[4,136,256]{2,1,0:T(8,128)S(1)}, u32[]{:S(2)}, u32[]{:S(2)}) async-start(f32[4,136,256]{2,1,0:T(8,128)} %broadcast_in_dim.63), calls=%async_computation.8 | async-start | bytes 1114112 | tf_op jit(solution)/shard_map/all_to_all | solution.py:74
Sparse Core Ops, SparseCore 0:
  10.8 85.9 all-gather.1
